TPU v7x, 256 devices: a whole 4x4x8 slice. The times are simulated.
256 devices in a mesh: seq: 8 (over x_hi, y), exp: 32 (over x_lo, z, core).
Axes of the slice: x: 4 (x_hi: 2, x_lo: 2; x = x_hi * 2 + x_lo), y: 4, z: 8, core: 2. Of those that a mesh axis runs over, the one named last changes fastest.
Arguments:
- tokens: bfloat16 [8192, 2560], P('exp'), may hold values from -6 to 6
- norm_gain: float32 [2560], replicated, may hold values from 0.1 to 1.9
- routes: int32 [8192, 6], P('exp'), may hold values from 0 to 63, all different within a row; in each aligned block of 256 rows (0 to 255, 256 to 511, ...) at most 25 rows name the same one
- route_weights: bfloat16 [8192, 6], P('exp'), may hold values from 0.049804688 to 0.3984375
- w_gate: bfloat16 [64, 2560, 1536], P('exp', None, 'seq'), may hold values from -0.125 to 0.125
- w_up: bfloat16 [64, 2560, 1536], P('exp', None, 'seq'), may hold values from -0.125 to 0.125
- w_down: bfloat16 [64, 1536, 2560], P('exp', 'seq'), may hold values from -0.15625 to 0.15625
- kv_prefill: bfloat16 [4, 2048, 32, 1024], P(None, ('seq', 'exp')), may hold values from -6 to 6
- block_map: int32 [2048], P(('seq', 'exp')), may hold values from 0 to 2047, as said below
- block_empty: int32 [2048], P(('seq', 'exp')), may hold values 0 or 1
Outputs:
- moe_out: bfloat16 [8192, 2560], P('exp', 'seq')
- kv_decode: bfloat16 [4, 2048, 32, 1024], P(None, ('seq', 'exp'))
Inputs may be any that keep to these rules, and one draw needn't show every extreme that they name: `routes`: in each aligned block of 256 rows no expert is named by more than 25 rows, a bound that some block reaches. block_map is a permutation of the 2048 blocks; a block keeps its index of exp, and each device sends exactly 1 block to each device of its seq group, itself included.
All inputs are finite; a program needn't handle non-finite values. No bound on the sum of `block_empty` on one device may be relied on, other than what follows from the above.
Results may differ from a plain program's by a relative error of at most 0.013.
Values may be sent and summed in bfloat16 or wider, within the bound.
No kernel may reach another device: no remote copies, remote signals or barrier semaphores. Data moves between devices by JAX's collectives and lax.ppermute only.
A program may use at most 128 MiB of HBM per device.

v0:
```python
import jax
import jax.numpy as jnp
from jax import lax
from jax.sharding import PartitionSpec as P


def passed_along(block, axis, distance):
    devices = range(lax.axis_size(axis))
    route = [((i - distance) % len(devices), i) for i in devices]
    return lax.ppermute(block, axis, route)


def rms_normed(tokens, norm_gain):
    values = tokens.astype(jnp.float32)
    scale = lax.rsqrt(jnp.mean(values * values, axis=-1, keepdims=True) + 1e-06)
    return (values * scale * norm_gain).astype(jnp.bfloat16)


def slot_layout(routes, experts, local_experts, owners, capacity):
    flat_routes = routes.reshape(-1)
    onehot = (flat_routes[:, None] == jnp.arange(experts, dtype=jnp.int32)[None, :]).astype(
        jnp.int32
    )
    before = jnp.cumsum(onehot, axis=0) - onehot
    position = jnp.sum(before * onehot, axis=1)
    owner = flat_routes // local_experts
    local_index = flat_routes % local_experts
    return (local_index * owners + owner) * capacity + position


def fill_slots(normed, slot_index, total_slots, topk):
    row_count = normed.shape[0]
    token_of = jnp.arange(slot_index.shape[0], dtype=jnp.int32) // topk
    source = jnp.full((total_slots,), row_count, jnp.int32).at[slot_index].set(token_of)
    padded = jnp.concatenate([normed, jnp.zeros((1, normed.shape[1]), normed.dtype)], axis=0)
    return padded[source]


def expert_block(rows, w_gate, w_up, w_down):
    gate = jnp.einsum("erd,edf->erf", rows, w_gate, preferred_element_type=jnp.float32)
    upward = jnp.einsum("erd,edf->erf", rows, w_up, preferred_element_type=jnp.float32)
    hidden = (jax.nn.silu(gate) * upward).astype(jnp.bfloat16)
    return jnp.einsum("erf,efd->erd", hidden, w_down, preferred_element_type=jnp.float32).astype(
        jnp.bfloat16
    )


def relayout(kv_prefill, block_map, block_empty):
    layers, blocks, block_rows, kv_width = kv_prefill.shape
    seq_count = lax.axis_size("seq")
    exp_count = lax.axis_size("exp")
    per_peer = blocks // seq_count
    keep = (1 - block_empty).astype(jnp.bfloat16)
    kept = kv_prefill * keep[None, :, None, None]
    peer = block_map // blocks // exp_count
    target = block_map % blocks
    order = jnp.argsort(peer * blocks + jnp.arange(blocks, dtype=jnp.int32))
    outgoing = kept[:, order].reshape(layers, seq_count, per_peer, block_rows, kv_width)
    labels = target[order].astype(jnp.bfloat16).reshape(1, seq_count, per_peer)
    my_seq = lax.axis_index("seq")
    arrived = outgoing
    tags = labels
    for step in range(1, seq_count):
        ahead = (my_seq + step) % seq_count
        piece = lax.dynamic_slice_in_dim(outgoing, ahead, 1, 1)
        label = lax.dynamic_slice_in_dim(labels, ahead, 1, 1)
        piece, label = passed_along((piece, label), "seq", step)
        behind = (my_seq - step + seq_count) % seq_count
        arrived = lax.dynamic_update_slice_in_dim(arrived, piece, behind, 1)
        tags = lax.dynamic_update_slice_in_dim(tags, label, behind, 1)
    arrived = arrived.reshape(layers, blocks, block_rows, kv_width)
    slots = tags.reshape(blocks).astype(jnp.int32)
    return arrived[:, jnp.argsort(slots)]


def per_device(
    tokens,
    norm_gain,
    routes,
    route_weights,
    w_gate,
    w_up,
    w_down,
    kv_prefill,
    block_map,
    block_empty,
):
    local_experts = w_gate.shape[0]
    exp_count = lax.axis_size("exp")
    experts = local_experts * exp_count
    tok_count, topk = routes.shape
    capacity = tok_count * topk // experts + 1
    normed = rms_normed(tokens, norm_gain)
    width = normed.shape[1]
    slot_index = slot_layout(routes, experts, local_experts, exp_count, capacity)
    total_slots = local_experts * exp_count * capacity
    outgoing = fill_slots(normed, slot_index, total_slots, topk).reshape(
        local_experts, exp_count * capacity, width
    )
    arrived = lax.all_to_all(outgoing, "exp", split_axis=1, concat_axis=1, tiled=True)
    partial_value = expert_block(arrived, w_gate, w_up, w_down)
    weights = route_weights.astype(jnp.float32)[:, :, None]
    returned = lax.all_to_all(
        partial_value, "exp", split_axis=1, concat_axis=1, tiled=True
    ).reshape(total_slots, width)
    picked = returned[slot_index].astype(jnp.float32).reshape(tok_count, topk, width)
    terms = jnp.sum(picked * weights, axis=1)
    mixed = lax.psum_scatter(terms.astype(jnp.bfloat16), "seq", scatter_dimension=1, tiled=True)
    kv_decode = relayout(kv_prefill, block_map, block_empty)
    return (mixed, kv_decode)


def solution(mesh):
    in_specs = (
        P("exp", None),
        P(),
        P("exp", None),
        P("exp", None),
        P("exp", None, "seq"),
        P("exp", None, "seq"),
        P("exp", "seq", None),
        P(None, ("seq", "exp"), None, None),
        P(("seq", "exp")),
        P(("seq", "exp")),
    )
    out_specs = (P("exp", "seq"), P(None, ("seq", "exp"), None, None))
    return jax.shard_map(
        per_device, mesh=mesh, in_specs=in_specs, out_specs=out_specs, check_vma=False
    )
```

profile of v0, /device:TPU:120, one launch (start us, length us, event | category | flops | bytes accessed | tf_op | source)
XLA Modules:
  0.0 717.7 jit_solution(14914148657757064392)
XLA Ops:
  7.2 1.0 copy.42
  8.6 1.7 fusion.4
  10.3 0.8 fusion.16
  11.1 34.6 %reduce-window.6 = s32[64,12,128]{2,1,0:T(8,128)} reduce-window(s32[64,12,128]{2,1,0:T(8,128)} %fusion.16, s32[]{:T(128)} %constant.187.clone.1), window={size=1x1x128 pad=0_0x0_0x127_0}, to_apply=%region_1.0 | reduce-window | flops 12484608 | bytes 786436 | tf_op jit(solution)/shard_map/reduce-window
  45.7 2.0 slice.18
  47.8 1.3 copy.45
  49.2 1.2 broadcast_add_fusion
  50.7 6.2 scatter_custom_fusion
  57.4 8.3 %gather_fusion = bf16[1600,2560]{1,0:T(8,128)(2,1)} fusion(bf16[257,2560]{1,0:T(8,128)(2,1)S(1)} %concatenate.3, s32[2048]{0:T(1024)S(1)} %pad_clamp_fusion.1), kind=kCustom, calls=%fused_computation | custom fusion | bytes 16390400 | tf_op jit(solution)/shard_map/gather | solution.py:36
  65.7 37.7 %copy.47 = bf16[2,800,2560]{2,0,1:T(2,128)(2,1)S(1)} copy(bf16[2,800,2560]{2,1,0:T(8,128)(2,1)} %bitcast.71) | data formatting | bytes 16384000 | tf_op jit(solution)/shard_map/reshape | solution.py:97
  103.3 188.8 %all_to_all.10 = bf16[2,800,2560]{2,0,1:T(2,128)(2,1)S(1)} all-to-all(bf16[2,800,2560]{2,0,1:T(2,128)(2,1)S(1)} %copy.47), channel_id=1, replica_groups=mesh['seq'=8,'exp'=32] {'exp'}, dimensions={1} | all-to-all | bytes 16384000 | tf_op jit(solution)/shard_map/all_to_all | solution.py:100
  292.1 3.2 copy-done.2
  295.3 4.2 fusion.2
  299.5 14.7 %convolution_convert_fusion = bf16[2,800,2560]{2,1,0:T(8,128)(2,1)} fusion(bf16[2,192,2560]{2,1,0:T(8,128)(2,1)S(1)} %copy-done, bf16[2,2560,192]{1,2,0:T(8,128)(2,1)} %param.15, bf16[2,800,2560]{2,0,1:T(2,128)(2,1)} %copy-done.2, f32[2,800,192]{1,2,0:T(8,128)} %fusion.2), kind=kOutput, calls=%fused_computation.11 | convolution fusion | flops 3151667200 | bytes 21544960 | tf_op jit(solution)/shard_map/erf,efd->erd/dot_general | solution.py:43
  314.2 38.5 %copy.50 = bf16[2,800,2560]{2,0,1:T(2,128)(2,1)} copy(bf16[2,800,2560]{2,1,0:T(8,128)(2,1)} %convolution_convert_fusion) | data formatting | bytes 16384000 | tf_op jit(solution)/shard_map/convert_element_type | solution.py:43
  352.7 7.3 %all-to-all-start.1 = ((bf16[2,800,2560]{2,0,1:T(2,128)(2,1)}), bf16[2,800,2560]{2,0,1:T(2,128)(2,1)}, u32[]{:S(2)}, u32[]{:S(2)}) async-start(bf16[2,800,2560]{2,0,1:T(2,128)(2,1)} %copy.50), calls=%async_computation.1 | async-start | bytes 16384000 | tf_op jit(solution)/shard_map/all_to_all | solution.py:103
  360.4 1.0 sort.31
  361.4 182.3 %all-to-all-done.1 = bf16[2,800,2560]{2,0,1:T(2,128)(2,1)} async-done(((bf16[2,800,2560]{2,0,1:T(2,128)(2,1)}), bf16[2,800,2560]{2,0,1:T(2,128)(2,1)}, u32[]{:S(2)}, u32[]{:S(2)}) %all-to-all-start.1) | async-done | bytes 8192032 | tf_op jit(solution)/shard_map/all_to_all | solution.py:103
  543.7 7.8 %copy.51 = bf16[2,800,2560]{2,1,0:T(8,128)(2,1)} copy(bf16[2,800,2560]{2,0,1:T(2,128)(2,1)} %all-to-all-done.1) | data formatting | bytes 16384000 | tf_op jit(solution)/shard_map/all_to_all | solution.py:103
  551.5 19.5 %gather_fusion.1 = bf16[1536,2560]{1,0:T(8,128)(2,1)} fusion(bf16[1600,2560]{1,0:T(8,128)(2,1)} %bitcast.70, s32[2048]{0:T(1024)S(1)} %pad_clamp_fusion), kind=kCustom, calls=%fused_computation.1 | custom fusion | bytes 15734784 | tf_op jit(solution)/shard_map/gather | solution.py:106
  571.0 14.2 %reshape.261 = f32[256,6,2560]{2,1,0:T(8,128)} reshape(bf16[1536,2560]{1,0:T(8,128)(2,1)} %gather_fusion.1) | data formatting | bytes 23592960 | tf_op jit(solution)/shard_map/convert_element_type | solution.py:106
  585.2 11.4 %multiply_reduce_fusion = bf16[256,2560]{1,0:T(8,128)(2,1)S(1)} fusion(f32[256,6,2560]{2,1,0:T(8,128)} %reshape.261, f32[256,6]{1,0:T(8,128)S(1)} %copy.52), kind=kLoop, calls=%fused_computation.6 | loop fusion | flops 7208960 | bytes 17045504 | tf_op jit(solution)/shard_map/reduce_sum | solution.py:107
  596.6 1.5 copy.56
  598.2 3.1 broadcast_multiply_fusion
  601.3 3.6 gather_fusion.2
  605.0 1.6 dynamic-slice_bitcast_fusion
  606.6 2.5 collective-permute-start
  609.0 2.6 collective-permute-start.1
  611.7 2.7 collective-permute-start.3
  615.1 0.7 fusion.29
  615.8 3.4 collective-permute-start.7
  619.2 22.8 %collective-permute-done.7 = bf16[1,1,1]{2,1,0:T(2,128)(2,1)} collective-permute-done((bf16[1,1,1]{2,1,0:T(2,128)(2,1)}, bf16[1,1,1]{2,1,0:T(2,128)(2,1)}, u32[]{:S(2)}, u32[]{:S(2)}) %collective-permute-start.7) | collective-permute-done | bytes 34 | tf_op jit(solution)/shard_map/ppermute | solution.py:10
  642.2 0.7 dynamic_update_slice.63
  643.0 4.5 collective-permute-done.8
  647.4 3.4 collective-permute-start.9
  650.8 0.8 dynamic_update_slice.64
  651.6 0.7 collective-permute-done.9
  652.4 5.8 collective-permute-start.10
  658.2 0.7 dynamic_update_slice.65
  658.8 0.9 collective-permute-done.10
  659.7 4.4 collective-permute-start.11
  664.2 0.7 dynamic_update_slice.66
  664.9 0.8 collective-permute-done.11
  665.7 4.4 collective-permute-start.12
  670.1 0.8 dynamic_update_slice.67
  670.9 2.4 collective-permute-done.12
  673.4 2.1 collective-permute-start.13
  675.5 0.8 dynamic_update_slice.68
  676.3 4.5 collective-permute-done.13
  681.7 1.0 sort.32
  682.7 1.3 collective-permute-start.5
  683.9 0.7 bitcast_dynamic-update-slice_fusion.6
  684.7 3.6 collective-permute-start.6
  688.3 0.7 bitcast_dynamic-update-slice_fusion.5
  689.0 0.7 bitcast_dynamic-update-slice_fusion.4
  689.7 0.7 bitcast_dynamic-update-slice_fusion.3
  690.4 0.7 bitcast_dynamic-update-slice_fusion.2
  691.1 4.0 collective-permute-done.5
  695.1 0.7 bitcast_dynamic-update-slice_fusion.1
  695.9 3.9 collective-permute-done.6
  699.7 0.7 bitcast_dynamic-update-slice_fusion
  700.5 3.2 copy.53
  703.7 3.6 gather_fusion.4
  707.3 3.3 copy.55
  (55 shorter events, 3.6 us)
Async XLA Ops:
  7.2 292.3 %copy-start = (bf16[2,192,2560]{2,1,0:T(8,128)(2,1)S(1)}, bf16[2,192,2560]{2,1,0:T(8,128)(2,1)}, u32[]{:S(2)}) copy-start(bf16[2,192,2560]{2,1,0:T(8,128)(2,1)} %param.16) | copy-start | bytes 5898244
  11.1 45.8 %copy-start.3 = (bf16[256,2560]{1,0:T(8,128)(2,1)S(1)}, bf16[256,2560]{1,0:T(8,128)(2,1)}, u32[]{:S(2)}) copy-start(bf16[256,2560]{1,0:T(8,128)(2,1)} %param.10) | copy-start | bytes 3932164
  11.1 45.8 %copy-start.4 = (f32[2560]{0:T(1024)S(1)}, f32[2560]{0:T(1024)}, u32[]{:S(2)}) copy-start(f32[2560]{0:T(1024)} %param.11) | copy-start | bytes 30724
  103.3 192.0 %copy-start.6 = (bf16[2,2560,192]{1,2,0:T(8,128)(2,1)S(1)}, bf16[2,2560,192]{1,2,0:T(8,128)(2,1)}, u32[]{:S(2)}) copy-start(bf16[2,2560,192]{1,2,0:T(8,128)(2,1)} %param.14) | copy-start | bytes 5898244
  292.1 3.2 copy-start.2
  352.7 7.6 %copy-start.5 = (bf16[256,6]{0,1:T(8,128)(2,1)S(1)}, bf16[256,6]{0,1:T(8,128)(2,1)}, u32[]{:S(2)}) copy-start(bf16[256,6]{0,1:T(8,128)(2,1)} %param.13) | copy-start | bytes 9220
  352.7 7.7 %copy-start.7 = (s32[8]{0:T(128)S(1)}, s32[8]{0:T(128)}, u32[]{:S(2)}) copy-start(s32[8]{0:T(128)} %param.18) | copy-start | bytes 100
  352.7 8.7 %copy-start.8 = (s32[8]{0:T(128)S(1)}, s32[8]{0:T(128)}, u32[]{:S(2)}) copy-start(s32[8]{0:T(128)} %param.19) | copy-start | bytes 100
  352.7 191.0 %all-to-all-start.1 = ((bf16[2,800,2560]{2,0,1:T(2,128)(2,1)}), bf16[2,800,2560]{2,0,1:T(2,128)(2,1)}, u32[]{:S(2)}, u32[]{:S(2)}) async-start(bf16[2,800,2560]{2,0,1:T(2,128)(2,1)} %copy.50), calls=%async_computation.1 | async-start | bytes 16384000 | tf_op jit(solution)/shard_map/all_to_all | solution.py:103
  360.0 350.6 %reduce-scatter.4.cloned.1.call-start = ((), (), s32[]{:S(2)}) async-start(), calls=%async_computation.3 | async-start | bytes 1474560
  606.6 76.1 %collective-permute-start = (bf16[4,1,1,32,1024]{4,3,0,2,1:T(8,128)(2,1)S(1)}, bf16[4,1,1,32,1024]{4,3,0,2,1:T(8,128)(2,1)S(1)}, u32[]{:S(2)}, u32[]{:S(2)}) collective-permute-start(bf16[4,1,1,32,1024]{4,3,0,2,1:T(8,128)(2,1)S(1)} %get-tuple-element.20), channel_id=1, source_target_pairs={{224,0},{0,32},{32,64},{64,96},{96,128},{128,160},{160,192},{192,2... | collective-permute-start | bytes 786440 | tf_op jit(solution)/shard_map/ppermute | solution.py:10
  609.0 75.6 %collective-permute-start.1 = (bf16[4,1,1,32,1024]{4,3,0,2,1:T(8,128)(2,1)S(1)}, bf16[4,1,1,32,1024]{4,3,0,2,1:T(8,128)(2,1)S(1)}, u32[]{:S(2)}, u32[]{:S(2)}) collective-permute-start(bf16[4,1,1,32,1024]{4,3,0,2,1:T(8,128)(2,1)S(1)} %get-tuple-element.19), channel_id=1, source_target_pairs={{192,0},{224,32},{0,64},{32,96},{64,128},{96,160},{128,192},{160,2... | collective-permute-start | bytes 786440 | tf_op jit(solution)/shard_map/ppermute | solution.py:10
  611.6 77.3 %collective-permute-start.2 = (bf16[4,1,1,32,1024]{4,3,0,2,1:T(8,128)(2,1)S(1)}, bf16[4,1,1,32,1024]{4,3,0,2,1:T(8,128)(2,1)S(1)}, u32[]{:S(2)}, u32[]{:S(2)}) collective-permute-start(bf16[4,1,1,32,1024]{4,3,0,2,1:T(8,128)(2,1)S(1)} %get-tuple-element.18), channel_id=1, source_target_pairs={{160,0},{192,32},{224,64},{0,96},{32,128},{64,160},{96,192},{128,2... | collective-permute-start | bytes 786440 | tf_op jit(solution)/shard_map/ppermute | solution.py:10
  611.7 78.0 %collective-permute-start.3 = (bf16[4,1,1,32,1024]{4,3,0,2,1:T(8,128)(2,1)S(1)}, bf16[4,1,1,32,1024]{4,3,0,2,1:T(8,128)(2,1)S(1)}, u32[]{:S(2)}, u32[]{:S(2)}) collective-permute-start(bf16[4,1,1,32,1024]{4,3,0,2,1:T(8,128)(2,1)S(1)} %get-tuple-element.17), channel_id=1, source_target_pairs={{128,0},{160,32},{192,64},{224,96},{0,128},{32,160},{64,192},{96,2... | collective-permute-start | bytes 786440 | tf_op jit(solution)/shard_map/ppermute | solution.py:10
  615.8 26.2 %collective-permute-start.7 = (bf16[1,1,1]{2,1,0:T(2,128)(2,1)}, bf16[1,1,1]{2,1,0:T(2,128)(2,1)}, u32[]{:S(2)}, u32[]{:S(2)}) collective-permute-start(bf16[1,1,1]{2,1,0:T(2,128)(2,1)} %bitcast.19), channel_id=1, source_target_pairs={{224,0},{0,32},{32,64},{64,96},{96,128},{128,160},{160,192},{192,2... | collective-permute-start | bytes 14 | tf_op jit(solution)/shard_map/ppermute | solution.py:10
  642.0 5.4 collective-permute-start.8
  647.4 4.9 collective-permute-start.9
  652.4 7.4 %collective-permute-start.10 = (bf16[1,1,1]{2,1,0:T(2,128)(2,1)}, bf16[1,1,1]{2,1,0:T(2,128)(2,1)}, u32[]{:S(2)}, u32[]{:S(2)}) collective-permute-start(bf16[1,1,1]{2,1,0:T(2,128)(2,1)} %bitcast.25), channel_id=1, source_target_pairs={{128,0},{160,32},{192,64},{224,96},{0,128},{32,160},{64,192},{96,2... | collective-permute-start | bytes 14 | tf_op jit(solution)/shard_map/ppermute | solution.py:10
  659.7 6.0 collective-permute-start.11
  665.7 7.6 %collective-permute-start.12 = (bf16[1,1,1]{2,1,0:T(2,128)(2,1)}, bf16[1,1,1]{2,1,0:T(2,128)(2,1)}, u32[]{:S(2)}, u32[]{:S(2)}) collective-permute-start(bf16[1,1,1]{2,1,0:T(2,128)(2,1)} %bitcast.29), channel_id=1, source_target_pairs={{64,0},{96,32},{128,64},{160,96},{192,128},{224,160},{0,192},{32,2... | collective-permute-start | bytes 14 | tf_op jit(solution)/shard_map/ppermute | solution.py:10
  673.4 7.4 %collective-permute-start.13 = (bf16[1,1,1]{2,1,0:T(2,128)(2,1)}, bf16[1,1,1]{2,1,0:T(2,128)(2,1)}, u32[]{:S(2)}, u32[]{:S(2)}) collective-permute-start(bf16[1,1,1]{2,1,0:T(2,128)(2,1)} %bitcast.31), channel_id=1, source_target_pairs={{32,0},{64,32},{96,64},{128,96},{160,128},{192,160},{224,192},{0,2... | collective-permute-start | bytes 14 | tf_op jit(solution)/shard_map/ppermute | solution.py:10
  680.8 9.6 %collective-permute-start.4 = (bf16[4,1,1,32,1024]{4,3,0,2,1:T(8,128)(2,1)S(1)}, bf16[4,1,1,32,1024]{4,3,0,2,1:T(8,128)(2,1)S(1)}, u32[]{:S(2)}, u32[]{:S(2)}) collective-permute-start(bf16[4,1,1,32,1024]{4,3,0,2,1:T(8,128)(2,1)S(1)} %get-tuple-element.16), channel_id=1, source_target_pairs={{96,0},{128,32},{160,64},{192,96},{224,128},{0,160},{32,192},{64,2... | collective-permute-start | bytes 786440 | tf_op jit(solution)/shard_map/ppermute | solution.py:10
  682.7 12.5 %collective-permute-start.5 = (bf16[4,1,1,32,1024]{4,3,0,2,1:T(8,128)(2,1)S(1)}, bf16[4,1,1,32,1024]{4,3,0,2,1:T(8,128)(2,1)S(1)}, u32[]{:S(2)}, u32[]{:S(2)}) collective-permute-start(bf16[4,1,1,32,1024]{4,3,0,2,1:T(8,128)(2,1)S(1)} %get-tuple-element.15), channel_id=1, source_target_pairs={{64,0},{96,32},{128,64},{160,96},{192,128},{224,160},{0,192},{32,2... | collective-permute-start | bytes 786440 | tf_op jit(solution)/shard_map/ppermute | solution.py:10
  684.7 15.1 %collective-permute-start.6 = (bf16[4,1,1,32,1024]{4,3,0,2,1:T(8,128)(2,1)S(1)}, bf16[4,1,1,32,1024]{4,3,0,2,1:T(8,128)(2,1)S(1)}, u32[]{:S(2)}, u32[]{:S(2)}) collective-permute-start(bf16[4,1,1,32,1024]{4,3,0,2,1:T(8,128)(2,1)S(1)} %get-tuple-element.14), channel_id=1, source_target_pairs={{32,0},{64,32},{96,64},{128,96},{160,128},{192,160},{224,192},{0,2... | collective-permute-start | bytes 786440 | tf_op jit(solution)/shard_map/ppermute | solution.py:10
  707.3 3.3 copy-start.1
Sparse Core Ops, SparseCore 0:
  598.2 89.1 reduce-scatter.3
where the time goes:
time: 727 us; the launch traced here: 718 us
  waiting for transfers between devices  227 us (31%)
  blocking collectives  189 us (26%)
  local copies, waits for them, and re-layouts  169 us (23%)
  other arithmetic  55.6 us (8%)
  starting transfers between devices  44.2 us (6%)
  matrix products  18.9 us (3%)
  between operations  14.6 us (2%)
    all_to_all x1, blocking collectives, per_device(): lax.all_to_all(outgoing, 'exp', split_axis=1, concat_axis=1, tiled=True)  189 us
    all_to_all x1, waiting for transfers between devices, per_device(): lax.all_to_all(partial_value, 'exp', split_axis=1, concat_axis=1, tiled=T...  182 us
    ppermute x14, waiting for transfers between devices, passed_along(): return lax.ppermute(block, axis, route)  44.5 us
    convert_element_type x1, local copies, waits for them, and re-layouts, expert_block(): jnp.einsum('erf,efd->erd', hidden, w_down, preferred_element_type=jnp.flo...  38.5 us
    reshape x1, local copies, waits for them, and re-layouts, per_device(): fill_slots(normed, slot_index, total_slots, topk)  37.7 us
    ppermute x14, starting transfers between devices, passed_along(): return lax.ppermute(block, axis, route)  36.7 us
    another operation x3, other arithmetic  35.9 us
    gather x1, local copies, waits for them, and re-layouts, per_device(): returned[slot_index].astype(jnp.float32).reshape(tok_count, topk, width)  19.5 us
  transfers between devices with their start and end apart: 16, of which 10 were waited for; matrix products, arithmetic and copies ran while one was open for 4% of the time, Pallas kernels for 0%

commit v1 on v0

--- a/solution.py
+++ b/solution.py
@@ -100,8 +100,11 @@
     arrived = lax.all_to_all(outgoing, "exp", split_axis=1, concat_axis=1, tiled=True)
     partial_value = expert_block(arrived, w_gate, w_up, w_down)
     weights = route_weights.astype(jnp.float32)[:, :, None]
-    returned = lax.all_to_all(
-        partial_value, "exp", split_axis=1, concat_axis=1, tiled=True
+    returned = jnp.concatenate(
+        lax.all_to_all(
+            jnp.stack(jnp.split(partial_value, lax.axis_size("exp"), axis=1)), "exp", 0, 0
+        ),
+        axis=1,
     ).reshape(total_slots, width)
     picked = returned[slot_index].astype(jnp.float32).reshape(tok_count, topk, width)
     terms = jnp.sum(picked * weights, axis=1)

time: 727 us -> 703 us (0.967)
  other arithmetic: 55.6 us -> 38.5 us
    convert_element_type x1 -> x0, local copies, waits for them, and re-layouts: 38.5 us -> none  [expert_block(): jnp.einsum('erf,efd->erd', hidden, w_down, preferred_element_type=jnp.flo...]
    another operation x1 -> x4, local copies, waits for them, and re-layouts: 0.1 us -> 18.4 us  [the longest x1 10.4 us: per_device(): returned = jnp.concatenate(lax.all_to_all(jnp.stack(jnp.split(partial_val...]
    another operation x3, other arithmetic: 35.9 us -> 18.4 us
    unnamed x21 -> x50, local copies, waits for them, and re-layouts: 8.98 us -> 24.6 us
    reshape x0 -> x1, local copies, waits for them, and re-layouts: none -> 9.53 us  [per_device(): jnp.concatenate(lax.all_to_all(jnp.stack(jnp.split(partial_value, lax.axi...]
    all_to_all x1 -> x0, local copies, waits for them, and re-layouts: 7.78 us -> none  [per_device(): lax.all_to_all(partial_value, 'exp', split_axis=1, concat_axis=1, tiled=T...]
  transfers between devices with their start and end apart: 16 -> 16, of which waited for: 10 -> 10; matrix products, arithmetic and copies ran while one was open for 4% -> 5% of each run, Pallas kernels for 0% -> 0%
where the time goes in v1:
time: 703 us; the launch traced here: 695 us
  waiting for transfers between devices  227 us (32%)
  blocking collectives  189 us (27%)
  local copies, waits for them, and re-layouts  164 us (23%)
  starting transfers between devices  43.9 us (6%)
  other arithmetic  38.5 us (5%)
  matrix products  18.8 us (3%)
  between operations  14.8 us (2%)
    all_to_all x1, blocking collectives, per_device(): lax.all_to_all(outgoing, 'exp', split_axis=1, concat_axis=1, tiled=True)  189 us
    all_to_all x1, waiting for transfers between devices, per_device(): lax.all_to_all(jnp.stack(jnp.split(partial_value, lax.axis_size('exp'), a...  182 us
    ppermute x14, waiting for transfers between devices, passed_along(): return lax.ppermute(block, axis, route)  44.3 us
    reshape x1, local copies, waits for them, and re-layouts, per_device(): fill_slots(normed, slot_index, total_slots, topk)  37.7 us
    ppermute x14, starting transfers between devices, passed_along(): return lax.ppermute(block, axis, route)  36.3 us
    unnamed x50, local copies, waits for them, and re-layouts  24.6 us
    gather x1, local copies, waits for them, and re-layouts, per_device(): returned[slot_index].astype(jnp.float32).reshape(tok_count, topk, width)  19.5 us
    another operation x3, other arithmetic  18.4 us
  transfers between devices with their start and end apart: 16, of which 10 were waited for; matrix products, arithmetic and copies ran while one was open for 5% of the time, Pallas kernels for 0%

profile of v1, /device:TPU:120, one launch (start us, length us, event | category | flops | bytes accessed | tf_op | source)
XLA Modules:
  0.0 695.4 jit_solution(96313104337102624)
XLA Ops:
  7.2 1.0 copy.44
  8.6 18.1 %reduce-window.6 = s32[64,12,128]{2,1,0:T(8,128)S(1)} reduce-window(s32[64,12,128]{2,1,0:T(8,128)S(1)} %fusion.16, s32[]{:T(128)} %constant.187.clone.1), window={size=1x1x128 pad=0_0x0_0x127_0}, to_apply=%region_1.0 | reduce-window | flops 12484608 | bytes 786436 | tf_op jit(solution)/shard_map/reduce-window
  27.9 6.2 scatter_custom_fusion
  34.1 1.7 fusion.4
  35.7 1.7 fusion.6
  37.5 8.3 %gather_fusion = bf16[1600,2560]{1,0:T(8,128)(2,1)} fusion(bf16[257,2560]{1,0:T(8,128)(2,1)S(1)} %concatenate.3, s32[2048]{0:T(1024)S(1)} %get-tuple-element.31), kind=kCustom, calls=%fused_computation | custom fusion | bytes 16390400 | tf_op jit(solution)/shard_map/gather | solution.py:36
  45.8 37.7 %copy.49 = bf16[2,800,2560]{2,0,1:T(2,128)(2,1)S(1)} copy(bf16[2,800,2560]{2,1,0:T(8,128)(2,1)} %bitcast.198) | data formatting | bytes 16384000 | tf_op jit(solution)/shard_map/reshape | solution.py:97
  83.5 188.8 %all_to_all.10 = bf16[2,800,2560]{2,0,1:T(2,128)(2,1)S(1)} all-to-all(bf16[2,800,2560]{2,0,1:T(2,128)(2,1)S(1)} %copy.49), channel_id=1, replica_groups=mesh['seq'=8,'exp'=32] {'exp'}, dimensions={1} | all-to-all | bytes 16384000 | tf_op jit(solution)/shard_map/all_to_all | solution.py:100
  272.3 3.1 copy-done.3
  275.4 4.2 fusion.2
  279.6 14.6 %convolution_convert_fusion = bf16[2,800,2560]{2,1,0:T(8,128)(2,1)} fusion(bf16[2,192,2560]{2,1,0:T(8,128)(2,1)S(1)} %copy-done, bf16[2,2560,192]{1,2,0:T(8,128)(2,1)} %param.15, bf16[2,800,2560]{2,0,1:T(2,128)(2,1)} %copy-done.3, f32[2,800,192]{1,2,0:T(8,128)} %fusion.2), kind=kOutput, calls=%fused_computation.11 | convolution fusion | flops 3151667200 | bytes 21544960 | tf_op jit(solution)/shard_map/erf,efd->erd/dot_general | solution.py:43
  294.2 1.1 fusion.51
  295.4 1.3 fusion.50
  296.7 1.2 fusion.49
  297.9 1.1 fusion.48
  299.0 1.1 fusion.47
  300.1 1.1 fusion.46
  301.1 1.1 fusion.45
  302.2 1.1 fusion.44
  303.3 1.0 fusion.43
  304.3 1.1 fusion.42
  305.4 1.1 fusion.41
  306.5 1.1 fusion.40
  307.6 1.1 fusion.39
  310.3 7.8 %copy.52 = bf16[32,2,25,2560]{3,1,2,0:T(2,128)(2,1)} copy(bf16[32,2,25,2560]{3,2,1,0:T(8,128)(2,1)S(1)} %fusion.20) | data formatting | bytes 16384000 | tf_op jit(solution)/shard_map/stack | solution.py:105
  318.2 7.3 %all-to-all-start.1 = ((bf16[32,2,25,2560]{3,1,2,0:T(2,128)(2,1)}), bf16[32,2,25,2560]{3,1,2,0:T(2,128)(2,1)}, u32[]{:S(2)}, u32[]{:S(2)}) async-start(bf16[32,2,25,2560]{3,1,2,0:T(2,128)(2,1)} %copy.52), calls=%async_computation.1 | async-start | bytes 16384000 | tf_op jit(solution)/shard_map/all_to_all | solution.py:104
  325.9 1.0 sort.31
  326.8 182.3 %all-to-all-done.1 = bf16[32,2,25,2560]{3,1,2,0:T(2,128)(2,1)} async-done(((bf16[32,2,25,2560]{3,1,2,0:T(2,128)(2,1)}), bf16[32,2,25,2560]{3,1,2,0:T(2,128)(2,1)}, u32[]{:S(2)}, u32[]{:S(2)}) %all-to-all-start.1) | async-done | bytes 8192032 | tf_op jit(solution)/shard_map/all_to_all | solution.py:104
  509.2 9.5 %copy.53 = bf16[2,32,25,2560]{3,2,1,0:T(8,128)(2,1)} copy(bf16[2,32,25,2560]{3,0,2,1:T(2,128)(2,1)} %bitcast.35) | data formatting | bytes 16384000 | tf_op jit(solution)/shard_map/reshape | solution.py:103
  518.7 10.4 %reshape_reshape.3 = bf16[1600,2560]{1,0:T(8,128)(2,1)} reshape(bf16[2,32,25,2560]{3,2,1,0:T(8,128)(2,1)} %copy.53) | data formatting | bytes 16384000 | tf_op jit(solution)/shard_map/reshape;reshape | solution.py:108
  529.1 19.5 %gather_fusion.1 = bf16[1536,2560]{1,0:T(8,128)(2,1)} fusion(bf16[1600,2560]{1,0:T(8,128)(2,1)} %reshape_reshape.3, s32[2048]{0:T(1024)S(1)} %get-tuple-element.30), kind=kCustom, calls=%fused_computation.1 | custom fusion | bytes 15734784 | tf_op jit(solution)/shard_map/gather | solution.py:109
  548.5 14.2 %reshape.261 = f32[256,6,2560]{2,1,0:T(8,128)} reshape(bf16[1536,2560]{1,0:T(8,128)(2,1)} %gather_fusion.1) | data formatting | bytes 23592960 | tf_op jit(solution)/shard_map/convert_element_type | solution.py:109
  562.8 11.4 %multiply_reduce_fusion = bf16[256,2560]{1,0:T(8,128)(2,1)S(1)} fusion(f32[256,6,2560]{2,1,0:T(8,128)} %reshape.261, f32[256,6]{1,0:T(8,128)S(1)} %copy.54), kind=kLoop, calls=%fused_computation.6 | loop fusion | flops 7208960 | bytes 17045504 | tf_op jit(solution)/shard_map/reduce_sum | solution.py:110
  574.2 1.5 copy.58
  575.8 3.1 broadcast_multiply_fusion
  578.9 3.6 gather_fusion.2
  582.5 2.6 dynamic-slice_bitcast_fusion
  585.1 2.4 collective-permute-start
  587.5 2.6 collective-permute-start.1
  590.2 2.7 collective-permute-start.3
  594.2 3.6 collective-permute-start.7
  597.8 21.8 %collective-permute-done.7 = bf16[1,1,1]{2,1,0:T(2,128)(2,1)} collective-permute-done((bf16[1,1,1]{2,1,0:T(2,128)(2,1)}, bf16[1,1,1]{2,1,0:T(2,128)(2,1)}, u32[]{:S(2)}, u32[]{:S(2)}) %collective-permute-start.7) | collective-permute-done | bytes 34 | tf_op jit(solution)/shard_map/ppermute | solution.py:10
  620.4 4.6 collective-permute-done.8
  625.0 3.3 collective-permute-start.9
  628.4 0.7 dynamic_update_slice.64
  629.1 0.9 collective-permute-done.9
  630.0 5.7 collective-permute-start.10
  636.4 1.0 collective-permute-done.10
  637.4 4.4 collective-permute-start.11
  642.6 1.0 collective-permute-done.11
  643.5 4.4 collective-permute-start.12
  648.6 2.4 collective-permute-done.12
  651.0 2.0 collective-permute-start.13
  653.0 0.8 dynamic_update_slice.68
  653.8 4.6 collective-permute-done.13
  658.7 0.7 dynamic_update_slice.69
  659.5 0.9 sort.32
  660.5 1.1 collective-permute-start.5
  662.3 3.6 collective-permute-start.6
  668.8 4.0 collective-permute-done.5
  673.6 4.0 collective-permute-done.6
  678.3 3.2 copy.55
  681.5 3.6 gather_fusion.4
  685.1 3.2 copy.57
  (85 shorter events, 13.3 us)
Async XLA Ops:
  7.2 272.4 %copy-start = (bf16[2,192,2560]{2,1,0:T(8,128)(2,1)S(1)}, bf16[2,192,2560]{2,1,0:T(8,128)(2,1)}, u32[]{:S(2)}) copy-start(bf16[2,192,2560]{2,1,0:T(8,128)(2,1)} %param.16) | copy-start | bytes 5898244
  83.5 192.0 %copy-start.5 = (bf16[2,2560,192]{1,2,0:T(8,128)(2,1)S(1)}, bf16[2,2560,192]{1,2,0:T(8,128)(2,1)}, u32[]{:S(2)}) copy-start(bf16[2,2560,192]{1,2,0:T(8,128)(2,1)} %param.14) | copy-start | bytes 5898244
  272.3 3.2 copy-start.3
  294.2 14.5 %copy-start.2 = (bf16[2,800,2560]{2,1,0:T(8,128)(2,1)S(1)}, bf16[2,800,2560]{2,1,0:T(8,128)(2,1)}, u32[]{:S(2)}) copy-start(bf16[2,800,2560]{2,1,0:T(8,128)(2,1)} %convolution_convert_fusion) | copy-start | bytes 24576004
  318.2 7.5 %copy-start.4 = (bf16[256,6]{0,1:T(8,128)(2,1)S(1)}, bf16[256,6]{0,1:T(8,128)(2,1)}, u32[]{:S(2)}) copy-start(bf16[256,6]{0,1:T(8,128)(2,1)} %param.13) | copy-start | bytes 9220
  318.2 7.7 %copy-start.6 = (s32[8]{0:T(128)S(1)}, s32[8]{0:T(128)}, u32[]{:S(2)}) copy-start(s32[8]{0:T(128)} %param.18) | copy-start | bytes 100
  318.2 191.0 %all-to-all-start.1 = ((bf16[32,2,25,2560]{3,1,2,0:T(2,128)(2,1)}), bf16[32,2,25,2560]{3,1,2,0:T(2,128)(2,1)}, u32[]{:S(2)}, u32[]{:S(2)}) async-start(bf16[32,2,25,2560]{3,1,2,0:T(2,128)(2,1)} %copy.52), calls=%async_computation.1 | async-start | bytes 16384000 | tf_op jit(solution)/shard_map/all_to_all | solution.py:104
  325.5 362.9 %reduce-scatter.4.cloned.1.call-start = ((), (), s32[]{:S(2)}) async-start(), calls=%async_computation.3 | async-start | bytes 1474560
  562.8 12.9 %copy-start.7 = (s32[8]{0:T(128)S(1)}, s32[8]{0:T(128)}, u32[]{:S(2)}) copy-start(s32[8]{0:T(128)} %param.19) | copy-start | bytes 100
  585.1 75.3 %collective-permute-start = (bf16[4,1,1,32,1024]{4,3,0,2,1:T(8,128)(2,1)}, bf16[4,1,1,32,1024]{4,3,0,2,1:T(8,128)(2,1)S(1)}, u32[]{:S(2)}, u32[]{:S(2)}) collective-permute-start(bf16[4,1,1,32,1024]{4,3,0,2,1:T(8,128)(2,1)} %get-tuple-element.20), channel_id=1, source_target_pairs={{224,0},{0,32},{32,64},{64,96},{96,128},{128,160},{160,192},{192,2... | collective-permute-start | bytes 786440 | tf_op jit(solution)/shard_map/ppermute | solution.py:10
  587.5 74.8 %collective-permute-start.1 = (bf16[4,1,1,32,1024]{4,3,0,2,1:T(8,128)(2,1)}, bf16[4,1,1,32,1024]{4,3,0,2,1:T(8,128)(2,1)S(1)}, u32[]{:S(2)}, u32[]{:S(2)}) collective-permute-start(bf16[4,1,1,32,1024]{4,3,0,2,1:T(8,128)(2,1)} %get-tuple-element.19), channel_id=1, source_target_pairs={{192,0},{224,32},{0,64},{32,96},{64,128},{96,160},{128,192},{160,2... | collective-permute-start | bytes 786440 | tf_op jit(solution)/shard_map/ppermute | solution.py:10
  590.1 76.5 %collective-permute-start.2 = (bf16[4,1,1,32,1024]{4,3,0,2,1:T(8,128)(2,1)}, bf16[4,1,1,32,1024]{4,3,0,2,1:T(8,128)(2,1)S(1)}, u32[]{:S(2)}, u32[]{:S(2)}) collective-permute-start(bf16[4,1,1,32,1024]{4,3,0,2,1:T(8,128)(2,1)} %get-tuple-element.18), channel_id=1, source_target_pairs={{160,0},{192,32},{224,64},{0,96},{32,128},{64,160},{96,192},{128,2... | collective-permute-start | bytes 786440 | tf_op jit(solution)/shard_map/ppermute | solution.py:10
  590.2 77.2 %collective-permute-start.3 = (bf16[4,1,1,32,1024]{4,3,0,2,1:T(8,128)(2,1)}, bf16[4,1,1,32,1024]{4,3,0,2,1:T(8,128)(2,1)S(1)}, u32[]{:S(2)}, u32[]{:S(2)}) collective-permute-start(bf16[4,1,1,32,1024]{4,3,0,2,1:T(8,128)(2,1)} %get-tuple-element.17), channel_id=1, source_target_pairs={{128,0},{160,32},{192,64},{224,96},{0,128},{32,160},{64,192},{96,2... | collective-permute-start | bytes 786440 | tf_op jit(solution)/shard_map/ppermute | solution.py:10
  592.9 95.4 %copy-start.1 = (bf16[2,192,2560]{2,1,0:T(8,128)(2,1)S(1)}, bf16[2,192,2560]{2,1,0:T(8,128)(2,1)}, u32[]{:S(2)}) copy-start(bf16[2,192,2560]{2,1,0:T(8,128)(2,1)} %param.16) | copy-start | bytes 5898244
  594.2 25.4 %collective-permute-start.7 = (bf16[1,1,1]{2,1,0:T(2,128)(2,1)}, bf16[1,1,1]{2,1,0:T(2,128)(2,1)}, u32[]{:S(2)}, u32[]{:S(2)}) collective-permute-start(bf16[1,1,1]{2,1,0:T(2,128)(2,1)} %bitcast.51), channel_id=1, source_target_pairs={{224,0},{0,32},{32,64},{64,96},{96,128},{128,160},{160,192},{192,2... | collective-permute-start | bytes 14 | tf_op jit(solution)/shard_map/ppermute | solution.py:10
  619.6 5.4 collective-permute-start.8
  625.0 4.9 collective-permute-start.9
  630.0 7.4 %collective-permute-start.10 = (bf16[1,1,1]{2,1,0:T(2,128)(2,1)}, bf16[1,1,1]{2,1,0:T(2,128)(2,1)}, u32[]{:S(2)}, u32[]{:S(2)}) collective-permute-start(bf16[1,1,1]{2,1,0:T(2,128)(2,1)} %bitcast.57), channel_id=1, source_target_pairs={{128,0},{160,32},{192,64},{224,96},{0,128},{32,160},{64,192},{96,2... | collective-permute-start | bytes 14 | tf_op jit(solution)/shard_map/ppermute | solution.py:10
  637.4 6.1 collective-permute-start.11
  643.5 7.5 %collective-permute-start.12 = (bf16[1,1,1]{2,1,0:T(2,128)(2,1)}, bf16[1,1,1]{2,1,0:T(2,128)(2,1)}, u32[]{:S(2)}, u32[]{:S(2)}) collective-permute-start(bf16[1,1,1]{2,1,0:T(2,128)(2,1)} %bitcast.61), channel_id=1, source_target_pairs={{64,0},{96,32},{128,64},{160,96},{192,128},{224,160},{0,192},{32,2... | collective-permute-start | bytes 14 | tf_op jit(solution)/shard_map/ppermute | solution.py:10
  651.0 7.3 %collective-permute-start.13 = (bf16[1,1,1]{2,1,0:T(2,128)(2,1)}, bf16[1,1,1]{2,1,0:T(2,128)(2,1)}, u32[]{:S(2)}, u32[]{:S(2)}) collective-permute-start(bf16[1,1,1]{2,1,0:T(2,128)(2,1)} %bitcast.63), channel_id=1, source_target_pairs={{32,0},{64,32},{96,64},{128,96},{160,128},{192,160},{224,192},{0,2... | collective-permute-start | bytes 14 | tf_op jit(solution)/shard_map/ppermute | solution.py:10
  658.4 9.7 %collective-permute-start.4 = (bf16[4,1,1,32,1024]{4,3,0,2,1:T(8,128)(2,1)}, bf16[4,1,1,32,1024]{4,3,0,2,1:T(8,128)(2,1)S(1)}, u32[]{:S(2)}, u32[]{:S(2)}) collective-permute-start(bf16[4,1,1,32,1024]{4,3,0,2,1:T(8,128)(2,1)} %get-tuple-element.16), channel_id=1, source_target_pairs={{96,0},{128,32},{160,64},{192,96},{224,128},{0,160},{32,192},{64,2... | collective-permute-start | bytes 786440 | tf_op jit(solution)/shard_map/ppermute | solution.py:10
  660.5 12.4 %collective-permute-start.5 = (bf16[4,1,1,32,1024]{4,3,0,2,1:T(8,128)(2,1)}, bf16[4,1,1,32,1024]{4,3,0,2,1:T(8,128)(2,1)S(1)}, u32[]{:S(2)}, u32[]{:S(2)}) collective-permute-start(bf16[4,1,1,32,1024]{4,3,0,2,1:T(8,128)(2,1)} %get-tuple-element.15), channel_id=1, source_target_pairs={{64,0},{96,32},{128,64},{160,96},{192,128},{224,160},{0,192},{32,2... | collective-permute-start | bytes 786440 | tf_op jit(solution)/shard_map/ppermute | solution.py:10
  662.3 15.3 %collective-permute-start.6 = (bf16[4,1,1,32,1024]{4,3,0,2,1:T(8,128)(2,1)S(1)}, bf16[4,1,1,32,1024]{4,3,0,2,1:T(8,128)(2,1)S(1)}, u32[]{:S(2)}, u32[]{:S(2)}) collective-permute-start(bf16[4,1,1,32,1024]{4,3,0,2,1:T(8,128)(2,1)S(1)} %get-tuple-element.14), channel_id=1, source_target_pairs={{32,0},{64,32},{96,64},{128,96},{160,128},{192,160},{224,192},{0,2... | collective-permute-start | bytes 786440 | tf_op jit(solution)/shard_map/ppermute | solution.py:10
Sparse Core Ops, SparseCore 0:
  575.8 89.6 reduce-scatter.3
